TPU v7x, 32 devices: a whole 2x2x4 slice. The times are simulated.
32 devices in a mesh: region: 2 (over y), mod: 4 (over z), obs: 4 (over x, core).
Axes of the slice: x: 2, y: 2, z: 4, core: 2. Of those that a mesh axis runs over, the one named last changes fastest.
Arguments:
- model_days: float32 [16384, 128], P(('region', 'mod')), parts along dimension 0, may hold values from -48 to 48
- obs_days: float32 [16384, 128], P(('region', 'obs', 'mod')), parts along dimension 0, may hold values from -48 to 48
Outputs:
- mapped: float32 [16384, 128], P(('region', 'mod', 'obs')), parts along dimension 0
- row_potential: float32 [16384], P(('region', 'mod')), parts along dimension 0
- col_potential: float32 [16384], P(('region', 'obs')), parts along dimension 0
There are 2 independent parts, one for each index of `region`. A program takes and returns all parts, laid end to end along the dimension named above; each array names one. Nothing has to cross between parts.
All inputs are finite; a program needn't handle non-finite values.
Results may differ from a plain program's by a relative error of at most 0.0003.
Values sent between devices are 32-bit elements; how exact they have to be, the bound alone decides.
No kernel may reach another device: no remote copies, remote signals or barrier semaphores. Data moves between devices by JAX's collectives and lax.ppermute only.
A program may use at most 64 MiB of HBM per device.

v0:
```python
import math
import jax
import jax.numpy as jnp
from jax import lax
from jax.sharding import PartitionSpec as P

ITERS = 2
entropy_scale = 0.02


def pair_cost(block_rows, block_square, columns):
    column_square = jnp.sum(columns * columns, axis=1)
    cross = lax.dot_general(
        block_rows,
        columns,
        (((1,), (1,)), ((), ())),
        precision=lax.Precision.HIGHEST,
        preferred_element_type=jnp.float32,
    )
    return (block_square[:, None] + column_square[None, :] - 2.0 * cross) / block_rows.shape[1]


def across_obs(peaks, totals):
    highest = lax.pmax(peaks, "obs")
    summed = lax.psum(totals * jnp.exp(peaks - highest), "obs")
    return highest + jnp.log(summed)


def across_mod(peaks, totals):
    highest = lax.pmax(peaks, "mod")
    summed = lax.psum(totals * jnp.exp(peaks - highest), "mod")
    return highest + jnp.log(summed)


def on_device(model_days, obs_days):
    row_square = jnp.sum(model_days * model_days, axis=1)
    row_count = model_days.shape[0]
    col_count = obs_days.shape[0] * lax.axis_size("mod")
    log_obs = math.log(col_count * lax.axis_size("obs"))
    log_model = math.log(row_count * lax.axis_size("mod"))
    gathered = lax.all_gather(obs_days, "mod", axis=0, tiled=True)
    cost_tile = pair_cost(model_days, row_square, gathered)

    def row_stats(col_potential):
        scores = (col_potential[None, :] - cost_tile) / entropy_scale
        peaks = jnp.max(scores, axis=1)
        return (peaks, jnp.sum(jnp.exp(scores - peaks[:, None]), axis=1))

    col_potential = jnp.zeros((col_count,), jnp.float32)
    for iteration in range(ITERS):
        peaks, totals = row_stats(col_potential)
        row_potential = -entropy_scale * (across_obs(peaks, totals) - log_obs)
        col_scores = (row_potential[:, None] - cost_tile) / entropy_scale
        col_peaks = jnp.max(col_scores, axis=0)
        peaks = col_peaks
        totals = jnp.sum(jnp.exp(col_scores - col_peaks[None, :]), axis=0)
        col_potential = -entropy_scale * (across_mod(peaks, totals) - log_model)
    peaks, totals = row_stats(col_potential)
    final_lse = across_obs(peaks, totals)
    row_potential = -entropy_scale * (final_lse - log_obs)
    weights = jnp.exp((col_potential[None, :] - cost_tile) / entropy_scale - final_lse[:, None])
    partial_map = jnp.dot(
        weights, gathered, precision=lax.Precision.HIGHEST, preferred_element_type=jnp.float32
    )
    summed_map = lax.psum(partial_map, "obs")
    share = row_count // lax.axis_size("obs")
    mapped = lax.dynamic_slice_in_dim(summed_map, lax.axis_index("obs") * share, share, 0)
    return (mapped, row_potential, col_potential)


def solution(mesh):
    in_specs = (P(("region", "mod"), None), P(("region", "obs", "mod"), None))
    out_specs = (P(("region", "mod", "obs"), None), P(("region", "mod")), P(("region", "obs")))
    return jax.shard_map(
        on_device, mesh=mesh, in_specs=in_specs, out_specs=out_specs, check_vma=False
    )
```

profile of v0, /device:TPU:0, one launch (start us, length us, event | category | flops | bytes accessed | tf_op | source)
XLA Modules:
  0.0 285.6 jit_solution(2504910936190339218)
XLA Ops:
  9.5 30.8 %all-gather.2.cloned.1.call-done = f32[2048,128]{1,0:T(8,128)} async-done(((f32[512,128]{1,0:T(8,128)}), f32[2048,128]{1,0:T(8,128)}) %all-gather.2.cloned.1.call-update) | async-done | bytes 1048592 | tf_op jit(solution)/shard_map/all_gather | solution.py:41
  41.9 20.6 %fusion.3 = (f32[2048]{0:T(1024)S(1)}, f32[2048,2048]{0,1:T(8,128)}) fusion(f32[2048,128]{1,0:T(8,128)} %param.2, f32[2048,128]{1,0:T(8,128)} %all-gather.2.cloned.1.call-done, f32[2048]{0:T(1024)S(1)} %multiply_reduce_fusion, f32[2048]{0:T(1024)S(1)} %multiply_reduce_fusion.1), kind=kOutput, calls=%fused_computation.14 | convolution fusion | flops 6471809024 | bytes 18898944 | tf_op jit(solution)/shard_map/dot_general | solution.py:13
  62.5 6.2 %pmax.35 = f32[2048]{0:T(1024)S(1)} all-reduce(f32[2048]{0:T(1024)S(1)} %get-tuple-element.5), channel_id=1, replica_groups=mesh['region'=2,'mod'=4,'obs'=4] {'obs'}, use_global_device_ids=true, to_apply=%region_3.0 | all-reduce | flops 2048 | bytes 16384 | tf_op jit(solution)/shard_map/pmax | solution.py:24
  68.6 9.1 %exponential_reduce_fusion.4 = f32[2048]{0:T(1024)S(1)} fusion(f32[2048,2048]{0,1:T(8,128)} %get-tuple-element.6, f32[2048]{0:T(1024)S(1)} %get-tuple-element.5), kind=kLoop, calls=%fused_computation.11 | loop fusion | flops 16775168 | bytes 16793600 | tf_op jit(solution)/shard_map/reduce_sum | solution.py:47
  77.7 6.4 %psum.42 = f32[2048]{0:T(1024)S(1)} all-reduce(f32[2048]{0:T(1024)S(1)} %exponential_multiply_fusion.4), channel_id=1, replica_groups=mesh['region'=2,'mod'=4,'obs'=4] {'obs'}, use_global_device_ids=true, to_apply=%region_5.0 | all-reduce | flops 2048 | bytes 16384 | tf_op jit(solution)/shard_map/psum | solution.py:25
  84.2 7.5 %fusion.4 = f32[2048]{0:T(1024)S(1)} fusion(f32[2048,2048]{0,1:T(8,128)} %get-tuple-element.6, f32[2048]{0:T(1024)S(1)} %add_multiply_fusion.4), kind=kLoop, calls=%fused_computation.15 | loop fusion | flops 12580864 | bytes 16793600 | tf_op jit(solution)/shard_map/reduce_max | solution.py:54
  91.7 8.0 %exponential_reduce_fusion.3 = f32[2048]{0:T(1024)S(1)} fusion(f32[2048,2048]{0,1:T(8,128)} %get-tuple-element.6, f32[2048]{0:T(1024)S(1)} %fusion.4, f32[2048]{0:T(1024)S(1)} %add_multiply_fusion.4), kind=kLoop, calls=%fused_computation.9 | loop fusion | flops 16775168 | bytes 16801792 | tf_op jit(solution)/shard_map/reduce_sum | solution.py:56
  99.7 11.0 %pmax.36 = f32[2048]{0:T(1024)S(1)} all-reduce(f32[2048]{0:T(1024)S(1)} %fusion.4), channel_id=1, replica_groups=mesh['region'=2,'mod'=4,'obs'=4] {'mod'}, use_global_device_ids=true, to_apply=%region_7.0 | all-reduce | flops 2048 | bytes 16384 | tf_op jit(solution)/shard_map/pmax | solution.py:30
  110.7 8.5 %psum.43 = f32[2048]{0:T(1024)S(1)} all-reduce(f32[2048]{0:T(1024)S(1)} %exponential_multiply_fusion.3), channel_id=1, replica_groups=mesh['region'=2,'mod'=4,'obs'=4] {'mod'}, use_global_device_ids=true, to_apply=%region_9.0 | all-reduce | flops 2048 | bytes 16384 | tf_op jit(solution)/shard_map/psum | solution.py:31
  119.2 7.5 %fusion.5 = f32[2048]{0:T(1024)S(1)} fusion(f32[2048,2048]{0,1:T(8,128)} %get-tuple-element.6, f32[2048]{0:T(1024)S(1)} %add_multiply_fusion.3), kind=kLoop, calls=%fused_computation.16 | loop fusion | flops 12580864 | bytes 16793600 | tf_op jit(solution)/shard_map/reduce_max | solution.py:46
  126.7 8.0 %exponential_reduce_fusion.2 = f32[2048]{0:T(1024)S(1)} fusion(f32[2048,2048]{0,1:T(8,128)} %get-tuple-element.6, f32[2048]{0:T(1024)S(1)} %fusion.5, f32[2048]{0:T(1024)S(1)} %add_multiply_fusion.3), kind=kLoop, calls=%fused_computation.7 | loop fusion | flops 16775168 | bytes 16801792 | tf_op jit(solution)/shard_map/reduce_sum | solution.py:47
  134.7 5.8 %pmax.37 = f32[2048]{0:T(1024)S(1)} all-reduce(f32[2048]{0:T(1024)S(1)} %fusion.5), channel_id=1, replica_groups=mesh['region'=2,'mod'=4,'obs'=4] {'obs'}, use_global_device_ids=true, to_apply=%region_11.0 | all-reduce | flops 2048 | bytes 16384 | tf_op jit(solution)/shard_map/pmax | solution.py:24
  140.5 6.3 %psum.44 = f32[2048]{0:T(1024)S(1)} all-reduce(f32[2048]{0:T(1024)S(1)} %exponential_multiply_fusion.2), channel_id=1, replica_groups=mesh['region'=2,'mod'=4,'obs'=4] {'obs'}, use_global_device_ids=true, to_apply=%region_13.0 | all-reduce | flops 2048 | bytes 16384 | tf_op jit(solution)/shard_map/psum | solution.py:25
  146.8 7.5 %fusion.6 = f32[2048]{0:T(1024)S(1)} fusion(f32[2048,2048]{0,1:T(8,128)} %get-tuple-element.6, f32[2048]{0:T(1024)S(1)} %add_multiply_fusion.2), kind=kLoop, calls=%fused_computation.17 | loop fusion | flops 12580864 | bytes 16793600 | tf_op jit(solution)/shard_map/reduce_max | solution.py:54
  154.4 8.0 %exponential_reduce_fusion.1 = f32[2048]{0:T(1024)S(1)} fusion(f32[2048,2048]{0,1:T(8,128)} %get-tuple-element.6, f32[2048]{0:T(1024)S(1)} %fusion.6, f32[2048]{0:T(1024)S(1)} %add_multiply_fusion.2), kind=kLoop, calls=%fused_computation.5 | loop fusion | flops 16775168 | bytes 16801792 | tf_op jit(solution)/shard_map/reduce_sum | solution.py:56
  162.3 10.2 %pmax.38 = f32[2048]{0:T(1024)S(1)} all-reduce(f32[2048]{0:T(1024)S(1)} %fusion.6), channel_id=1, replica_groups=mesh['region'=2,'mod'=4,'obs'=4] {'mod'}, use_global_device_ids=true, to_apply=%region_15.0 | all-reduce | flops 2048 | bytes 16384 | tf_op jit(solution)/shard_map/pmax | solution.py:30
  172.6 9.0 %psum.45 = f32[2048]{0:T(1024)S(1)} all-reduce(f32[2048]{0:T(1024)S(1)} %exponential_multiply_fusion.1), channel_id=1, replica_groups=mesh['region'=2,'mod'=4,'obs'=4] {'mod'}, use_global_device_ids=true, to_apply=%region_17.0 | all-reduce | flops 2048 | bytes 16384 | tf_op jit(solution)/shard_map/psum | solution.py:31
  181.7 7.6 %fusion.7 = f32[2048]{0:T(1024)S(1)} fusion(f32[2048,2048]{0,1:T(8,128)} %get-tuple-element.6, f32[2048]{0:T(1024)S(1)} %add_multiply_fusion.1), kind=kLoop, calls=%fused_computation.18 | loop fusion | flops 12580864 | bytes 16793600 | tf_op jit(solution)/shard_map/reduce_max | solution.py:46
  189.2 8.0 %exponential_reduce_fusion = f32[2048]{0:T(1024)S(1)} fusion(f32[2048,2048]{0,1:T(8,128)} %get-tuple-element.6, f32[2048]{0:T(1024)S(1)} %fusion.7, f32[2048]{0:T(1024)S(1)} %add_multiply_fusion.1), kind=kLoop, calls=%fused_computation.3 | loop fusion | flops 16775168 | bytes 16801792 | tf_op jit(solution)/shard_map/reduce_sum | solution.py:47
  197.2 5.8 %pmax.39 = f32[2048]{0:T(1024)S(1)} all-reduce(f32[2048]{0:T(1024)S(1)} %fusion.7), channel_id=1, replica_groups=mesh['region'=2,'mod'=4,'obs'=4] {'obs'}, use_global_device_ids=true, to_apply=%region_19.0 | all-reduce | flops 2048 | bytes 16384 | tf_op jit(solution)/shard_map/pmax | solution.py:24
  203.0 6.9 %psum.46 = f32[2048]{0:T(1024)S(1)} all-reduce(f32[2048]{0:T(1024)S(1)} %exponential_multiply_fusion), channel_id=1, replica_groups=mesh['region'=2,'mod'=4,'obs'=4] {'obs'}, use_global_device_ids=true, to_apply=%region_21.0 | all-reduce | flops 2048 | bytes 16384 | tf_op jit(solution)/shard_map/psum | solution.py:25
  210.5 31.6 %fusion = f32[2048,128]{1,0:T(8,128)} fusion(f32[2048,128]{1,0:T(8,128)S(1)} %copy-done, f32[2048,2048]{0,1:T(8,128)} %get-tuple-element.6, f32[2048]{0:T(1024)S(1)} %get-tuple-element.4, f32[2048]{0:T(1024)S(1)} %add_multiply_fusion.1), kind=kOutput, calls=%fused_computation | convolution fusion | flops 6455033856 | bytes 18890752 | tf_op jit(solution)/shard_map/dot_general | solution.py:62
  242.1 34.9 %all-reduce.2.cloned.1.call-done = f32[2048,128]{1,0:T(8,128)} async-done(((f32[2048,128]{1,0:T(8,128)}), f32[2048,128]{1,0:T(8,128)}) %all-reduce.2.cloned.1.call-update) | async-done | bytes 1048592 | tf_op jit(solution)/shard_map/psum | solution.py:65
  277.0 1.7 constant_dynamic-slice_fusion
  (20 shorter events, 4.6 us)
Async XLA Ops:
  7.2 33.1 %all-gather.2.cloned.1.call-start = ((), (), s32[]{:S(2)}) async-start(), calls=%async_computation | async-start | bytes 1310720 | tf_op jit(solution)/shard_map/all_gather | solution.py:41
  7.9 269.1 %all-reduce.2.cloned.1.call-start = ((), (), s32[]{:S(2)}) async-start(), calls=%async_computation.1 | async-start | bytes 2097152 | tf_op jit(solution)/shard_map/psum | solution.py:65
  181.7 28.9 %copy-start.1 = (f32[2048]{0:T(1024)}, f32[2048]{0:T(1024)S(1)}, u32[]{:S(2)}) copy-start(f32[2048]{0:T(1024)S(1)} %add_multiply_fusion.1) | copy-start | bytes 24580
  181.7 28.8 %copy-start = (f32[2048,128]{1,0:T(8,128)S(1)}, f32[2048,128]{1,0:T(8,128)}, u32[]{:S(2)}) copy-start(f32[2048,128]{1,0:T(8,128)} %all-gather.2.cloned.1.call-done) | copy-start | bytes 3145732
Sparse Core Ops, SparseCore 0:
  9.5 30.6 all-gather.1
  242.2 34.7 all-reduce.1
where the time goes:
time: 286 us
  blocking collectives  76.1 us (27%)
  other arithmetic  74.9 us (26%)
  waiting for transfers between devices  66.4 us (23%)
  matrix products  52.2 us (18%)
  between operations  14.2 us (5%)
    psum x1, waiting for transfers between devices, on_device(): summed_map = lax.psum(partial_map, 'obs')  34.9 us
    dot_general x1, matrix products, on_device(): jnp.dot(weights, gathered, precision=lax.Precision.HIGHEST, preferred_ele...  31.6 us
    all_gather x1, waiting for transfers between devices, on_device(): gathered = lax.all_gather(obs_days, 'mod', axis=0, tiled=True)  30.8 us
    reduce_sum x3, other arithmetic, row_stats(): return (peaks, jnp.sum(jnp.exp(scores - peaks[:, None]), axis=1))  25 us
    pmax x2, blocking collectives, across_mod(): highest = lax.pmax(peaks, 'mod')  21.2 us
    dot_general x1, matrix products, pair_cost(): lax.dot_general(block_rows, columns, (((1,), (1,)), ((), ())), precision=...  20.6 us
    psum x3, blocking collectives, across_obs(): summed = lax.psum(totals * jnp.exp(peaks - highest), 'obs')  19.7 us
    pmax x3, blocking collectives, across_obs(): highest = lax.pmax(peaks, 'obs')  17.7 us
  transfers between devices with their start and end apart: 2, of which 2 were waited for; matrix products, arithmetic and copies ran while one was open for 1% of the time, Pallas kernels for 0%

commit v1 on v0

--- a/solution.py
+++ b/solution.py
@@ -6,6 +6,12 @@
 
 ITERS = 2
 entropy_scale = 0.02
+
+
+def joined_along(blocks, dim):
+    blocks = jnp.moveaxis(blocks, 0, dim)
+    shape = blocks.shape
+    return blocks.reshape(*shape[:dim], shape[dim] * shape[dim + 1], *shape[dim + 2 :])
 
 
 def pair_cost(block_rows, block_square, columns):
@@ -38,7 +44,19 @@
     col_count = obs_days.shape[0] * lax.axis_size("mod")
     log_obs = math.log(col_count * lax.axis_size("obs"))
     log_model = math.log(row_count * lax.axis_size("mod"))
-    gathered = lax.all_gather(obs_days, "mod", axis=0, tiled=True)
+    count = lax.axis_size("mod")
+    pairs = [(i, (i + 1) % count) for i in range(count)]
+    back = [(b, a) for a, b in pairs]
+    lower, upper = ([], [])
+    for step in range(count - 1):
+        if step % 2 == 0:
+            lower.append(lax.ppermute(lower[-1] if lower else obs_days, "mod", pairs))
+        else:
+            upper.append(lax.ppermute(upper[-1] if upper else obs_days, "mod", back))
+    blocks = jnp.stack([*lower[::-1], obs_days, *upper])
+    shift = lax.axis_index("mod") - len(lower)
+    blocks = blocks[(jnp.arange(count) - shift) % count]
+    gathered = joined_along(blocks, 0)
     cost_tile = pair_cost(model_days, row_square, gathered)
 
     def row_stats(col_potential):

time: 286 us -> 275 us (0.962)
  waiting for transfers between devices: 66.4 us -> 51.5 us
  starting transfers between devices: 0.08 us -> 5.24 us
    all_gather x1 -> x0, waiting for transfers between devices: 30.8 us -> none  [on_device(): gathered = lax.all_gather(obs_days, 'mod', axis=0, tiled=True)]
    ppermute x0 -> x3, waiting for transfers between devices: none -> 16.1 us  [the longest x2 13.3 us: on_device(): lower.append(lax.ppermute(lower[-1] if lower else obs_days, 'mod', pairs))]
    ppermute x0 -> x3, starting transfers between devices: none -> 5.2 us  [the longest x2 3.11 us: on_device(): lower.append(lax.ppermute(lower[-1] if lower else obs_days, 'mod', pairs))]
  transfers between devices with their start and end apart: 2 -> 4, of which waited for: 2 -> 4; matrix products, arithmetic and copies ran while one was open for 1% -> 1% of each run, Pallas kernels for 0% -> 0%
where the time goes in v1:
time: 275 us
  blocking collectives  75.6 us (27%)
  other arithmetic  74.6 us (27%)
  waiting for transfers between devices  51.5 us (19%)
  matrix products  51 us (19%)
  between operations  14.2 us (5%)
  starting transfers between devices  5.24 us (2%)
    psum x1, waiting for transfers between devices, on_device(): summed_map = lax.psum(partial_map, 'obs')  35.3 us
    dot_general x1, matrix products, on_device(): jnp.dot(weights, gathered, precision=lax.Precision.HIGHEST, preferred_ele...  31.5 us
    reduce_sum x3, other arithmetic, row_stats(): return (peaks, jnp.sum(jnp.exp(scores - peaks[:, None]), axis=1))  25 us
    pmax x2, blocking collectives, across_mod(): highest = lax.pmax(peaks, 'mod')  20.6 us
    psum x3, blocking collectives, across_obs(): summed = lax.psum(totals * jnp.exp(peaks - highest), 'obs')  20 us
    dot_general x1, matrix products, pair_cost(): lax.dot_general(block_rows, columns, (((1,), (1,)), ((), ())), precision=...  19.6 us
    psum x2, blocking collectives, across_mod(): summed = lax.psum(totals * jnp.exp(peaks - highest), 'mod')  17.5 us
    pmax x3, blocking collectives, across_obs(): highest = lax.pmax(peaks, 'obs')  17.5 us
  transfers between devices with their start and end apart: 4, of which 4 were waited for; matrix products, arithmetic and copies ran while one was open for 1% of the time, Pallas kernels for 0%

profile of v1, /device:TPU:0, one launch (start us, length us, event | category | flops | bytes accessed | tf_op | source)
XLA Modules:
  0.0 274.5 jit_solution(16848903617358490956)
XLA Ops:
  12.4 7.3 %collective-permute-done = f32[512,128]{1,0:T(8,128)S(1)} collective-permute-done((f32[512,128]{1,0:T(8,128)}, f32[512,128]{1,0:T(8,128)S(1)}, u32[]{:S(2)}, u32[]{:S(2)}) %collective-permute-start) | collective-permute-done | bytes 262176 | tf_op jit(solution)/shard_map/ppermute | solution.py:53
  24.1 6.0 %collective-permute-done.1 = f32[512,128]{1,0:T(8,128)S(1)} collective-permute-done((f32[512,128]{1,0:T(8,128)S(1)}, f32[512,128]{1,0:T(8,128)S(1)}, u32[]{:S(2)}, u32[]{:S(2)}) %collective-permute-start.1) | collective-permute-done | bytes 262176 | tf_op jit(solution)/shard_map/ppermute | solution.py:53
  32.1 19.6 %fusion.4 = (f32[2048]{0:T(1024)S(1)}, f32[2048,2048]{0,1:T(8,128)}) fusion(f32[2048,128]{1,0:T(8,128)S(1)} %bitcast.16, f32[2048,128]{1,0:T(8,128)} %param.2, f32[2048]{0:T(1024)S(1)} %bitcast.23, f32[2048]{0:T(1024)S(1)} %multiply_reduce_fusion.1), kind=kOutput, calls=%fused_computation.16 | convolution fusion | flops 6471809024 | bytes 18898944 | tf_op jit(solution)/shard_map/dot_general | solution.py:19
  51.7 5.7 %pmax.35 = f32[2048]{0:T(1024)S(1)} all-reduce(f32[2048]{0:T(1024)S(1)} %get-tuple-element.5), channel_id=1, replica_groups=mesh['region'=2,'mod'=4,'obs'=4] {'obs'}, use_global_device_ids=true, to_apply=%region_3.4 | all-reduce | flops 2048 | bytes 16384 | tf_op jit(solution)/shard_map/pmax | solution.py:30
  57.5 9.1 %exponential_reduce_fusion.4 = f32[2048]{0:T(1024)S(1)} fusion(f32[2048,2048]{0,1:T(8,128)} %get-tuple-element.6, f32[2048]{0:T(1024)S(1)} %get-tuple-element.5), kind=kLoop, calls=%fused_computation.14 | loop fusion | flops 16775168 | bytes 16793600 | tf_op jit(solution)/shard_map/reduce_sum | solution.py:65
  66.5 6.9 %psum.42 = f32[2048]{0:T(1024)S(1)} all-reduce(f32[2048]{0:T(1024)S(1)} %exponential_multiply_fusion.4), channel_id=1, replica_groups=mesh['region'=2,'mod'=4,'obs'=4] {'obs'}, use_global_device_ids=true, to_apply=%region_5.6 | all-reduce | flops 2048 | bytes 16384 | tf_op jit(solution)/shard_map/psum | solution.py:31
  73.4 7.5 %fusion.5 = f32[2048]{0:T(1024)S(1)} fusion(f32[2048,2048]{0,1:T(8,128)} %get-tuple-element.6, f32[2048]{0:T(1024)S(1)} %add_multiply_fusion.4), kind=kLoop, calls=%fused_computation.17 | loop fusion | flops 12580864 | bytes 16793600 | tf_op jit(solution)/shard_map/reduce_max | solution.py:72
  81.0 8.0 %exponential_reduce_fusion.3 = f32[2048]{0:T(1024)S(1)} fusion(f32[2048,2048]{0,1:T(8,128)} %get-tuple-element.6, f32[2048]{0:T(1024)S(1)} %fusion.5, f32[2048]{0:T(1024)S(1)} %add_multiply_fusion.4), kind=kLoop, calls=%fused_computation.12 | loop fusion | flops 16775168 | bytes 16801792 | tf_op jit(solution)/shard_map/reduce_sum | solution.py:74
  89.0 10.3 %pmax.36 = f32[2048]{0:T(1024)S(1)} all-reduce(f32[2048]{0:T(1024)S(1)} %fusion.5), channel_id=1, replica_groups=mesh['region'=2,'mod'=4,'obs'=4] {'mod'}, use_global_device_ids=true, to_apply=%region_7.8 | all-reduce | flops 2048 | bytes 16384 | tf_op jit(solution)/shard_map/pmax | solution.py:36
  99.2 8.8 %psum.43 = f32[2048]{0:T(1024)S(1)} all-reduce(f32[2048]{0:T(1024)S(1)} %exponential_multiply_fusion.3), channel_id=1, replica_groups=mesh['region'=2,'mod'=4,'obs'=4] {'mod'}, use_global_device_ids=true, to_apply=%region_9.10 | all-reduce | flops 2048 | bytes 16384 | tf_op jit(solution)/shard_map/psum | solution.py:37
  108.1 7.5 %fusion.6 = f32[2048]{0:T(1024)S(1)} fusion(f32[2048,2048]{0,1:T(8,128)} %get-tuple-element.6, f32[2048]{0:T(1024)S(1)} %add_multiply_fusion.3), kind=kLoop, calls=%fused_computation.18 | loop fusion | flops 12580864 | bytes 16793600 | tf_op jit(solution)/shard_map/reduce_max | solution.py:64
  115.5 8.0 %exponential_reduce_fusion.2 = f32[2048]{0:T(1024)S(1)} fusion(f32[2048,2048]{0,1:T(8,128)} %get-tuple-element.6, f32[2048]{0:T(1024)S(1)} %fusion.6, f32[2048]{0:T(1024)S(1)} %add_multiply_fusion.3), kind=kLoop, calls=%fused_computation.10 | loop fusion | flops 16775168 | bytes 16801792 | tf_op jit(solution)/shard_map/reduce_sum | solution.py:65
  123.5 5.8 %pmax.37 = f32[2048]{0:T(1024)S(1)} all-reduce(f32[2048]{0:T(1024)S(1)} %fusion.6), channel_id=1, replica_groups=mesh['region'=2,'mod'=4,'obs'=4] {'obs'}, use_global_device_ids=true, to_apply=%region_11.12 | all-reduce | flops 2048 | bytes 16384 | tf_op jit(solution)/shard_map/pmax | solution.py:30
  129.3 6.5 %psum.44 = f32[2048]{0:T(1024)S(1)} all-reduce(f32[2048]{0:T(1024)S(1)} %exponential_multiply_fusion.2), channel_id=1, replica_groups=mesh['region'=2,'mod'=4,'obs'=4] {'obs'}, use_global_device_ids=true, to_apply=%region_13.14 | all-reduce | flops 2048 | bytes 16384 | tf_op jit(solution)/shard_map/psum | solution.py:31
  135.8 7.5 %fusion.7 = f32[2048]{0:T(1024)S(1)} fusion(f32[2048,2048]{0,1:T(8,128)} %get-tuple-element.6, f32[2048]{0:T(1024)S(1)} %add_multiply_fusion.2), kind=kLoop, calls=%fused_computation.19 | loop fusion | flops 12580864 | bytes 16793600 | tf_op jit(solution)/shard_map/reduce_max | solution.py:72
  143.4 8.0 %exponential_reduce_fusion.1 = f32[2048]{0:T(1024)S(1)} fusion(f32[2048,2048]{0,1:T(8,128)} %get-tuple-element.6, f32[2048]{0:T(1024)S(1)} %fusion.7, f32[2048]{0:T(1024)S(1)} %add_multiply_fusion.2), kind=kLoop, calls=%fused_computation.8 | loop fusion | flops 16775168 | bytes 16801792 | tf_op jit(solution)/shard_map/reduce_sum | solution.py:74
  151.4 10.3 %pmax.38 = f32[2048]{0:T(1024)S(1)} all-reduce(f32[2048]{0:T(1024)S(1)} %fusion.7), channel_id=1, replica_groups=mesh['region'=2,'mod'=4,'obs'=4] {'mod'}, use_global_device_ids=true, to_apply=%region_15.16 | all-reduce | flops 2048 | bytes 16384 | tf_op jit(solution)/shard_map/pmax | solution.py:36
  161.7 8.7 %psum.45 = f32[2048]{0:T(1024)S(1)} all-reduce(f32[2048]{0:T(1024)S(1)} %exponential_multiply_fusion.1), channel_id=1, replica_groups=mesh['region'=2,'mod'=4,'obs'=4] {'mod'}, use_global_device_ids=true, to_apply=%region_17.18 | all-reduce | flops 2048 | bytes 16384 | tf_op jit(solution)/shard_map/psum | solution.py:37
  170.5 7.5 %fusion.8 = f32[2048]{0:T(1024)S(1)} fusion(f32[2048,2048]{0,1:T(8,128)} %get-tuple-element.6, f32[2048]{0:T(1024)S(1)} %add_multiply_fusion.1), kind=kLoop, calls=%fused_computation.20 | loop fusion | flops 12580864 | bytes 16793600 | tf_op jit(solution)/shard_map/reduce_max | solution.py:64
  177.9 6.0 %pmax.39 = f32[2048]{0:T(1024)S(1)} all-reduce(f32[2048]{0:T(1024)S(1)} %fusion.8), channel_id=1, replica_groups=mesh['region'=2,'mod'=4,'obs'=4] {'obs'}, use_global_device_ids=true, to_apply=%region_19.20 | all-reduce | flops 2048 | bytes 16384 | tf_op jit(solution)/shard_map/pmax | solution.py:30
  183.9 8.0 %exponential_reduce_fusion = f32[2048]{0:T(1024)S(1)} fusion(f32[2048,2048]{0,1:T(8,128)} %get-tuple-element.6, f32[2048]{0:T(1024)S(1)} %fusion.8, f32[2048]{0:T(1024)S(1)} %add_multiply_fusion.1), kind=kLoop, calls=%fused_computation.6 | loop fusion | flops 16775168 | bytes 16801792 | tf_op jit(solution)/shard_map/reduce_sum | solution.py:65
  191.9 6.6 %psum.46 = f32[2048]{0:T(1024)S(1)} all-reduce(f32[2048]{0:T(1024)S(1)} %exponential_multiply_fusion), channel_id=1, replica_groups=mesh['region'=2,'mod'=4,'obs'=4] {'obs'}, use_global_device_ids=true, to_apply=%region_21.22 | all-reduce | flops 2048 | bytes 16384 | tf_op jit(solution)/shard_map/psum | solution.py:31
  199.2 31.5 %fusion.1 = f32[2048,128]{1,0:T(8,128)} fusion(f32[2048,128]{1,0:T(8,128)S(1)} %bitcast.17, f32[2048,2048]{0,1:T(8,128)} %get-tuple-element.6, f32[2048]{0:T(1024)S(1)} %get-tuple-element.4, f32[2048]{0:T(1024)S(1)} %add_multiply_fusion.1), kind=kOutput, calls=%fused_computation.3 | convolution fusion | flops 6455033856 | bytes 18890752 | tf_op jit(solution)/shard_map/dot_general | solution.py:80
  230.7 35.3 %all-reduce.2.cloned.1.call-done = f32[2048,128]{1,0:T(8,128)} async-done(((f32[2048,128]{1,0:T(8,128)}), f32[2048,128]{1,0:T(8,128)}) %all-reduce.2.cloned.1.call-update) | async-done | bytes 1048592 | tf_op jit(solution)/shard_map/psum | solution.py:83
  (26 shorter events, 14.0 us)
Async XLA Ops:
  7.2 258.8 %all-reduce.2.cloned.1.call-start = ((), (), s32[]{:S(2)}) async-start(), calls=%async_computation | async-start | bytes 2097152 | tf_op jit(solution)/shard_map/psum | solution.py:83
  7.2 12.5 %collective-permute-start = (f32[512,128]{1,0:T(8,128)}, f32[512,128]{1,0:T(8,128)S(1)}, u32[]{:S(2)}, u32[]{:S(2)}) collective-permute-start(f32[512,128]{1,0:T(8,128)} %param.3), channel_id=1, source_target_pairs={{0,4},{4,8},{8,12},{12,0},{1,5},{5,9},{9,13},{13,1},{2,6},{6,10},{... | collective-permute-start | bytes 786440 | tf_op jit(solution)/shard_map/ppermute | solution.py:53
  10.3 13.8 %collective-permute-start.2 = (f32[512,128]{1,0:T(8,128)}, f32[512,128]{1,0:T(8,128)S(1)}, u32[]{:S(2)}, u32[]{:S(2)}) collective-permute-start(f32[512,128]{1,0:T(8,128)} %param.3), channel_id=1, source_target_pairs={{4,0},{8,4},{12,8},{0,12},{5,1},{9,5},{13,9},{1,13},{6,2},{10,6},{... | collective-permute-start | bytes 786440 | tf_op jit(solution)/shard_map/ppermute | solution.py:55
  19.8 10.4 %collective-permute-start.1 = (f32[512,128]{1,0:T(8,128)S(1)}, f32[512,128]{1,0:T(8,128)S(1)}, u32[]{:S(2)}, u32[]{:S(2)}) collective-permute-start(f32[512,128]{1,0:T(8,128)S(1)} %collective-permute-done), channel_id=1, source_target_pairs={{0,4},{4,8},{8,12},{12,0},{1,5},{5,9},{9,13},{13,1},{2,6},{6,10},{... | collective-permute-start | bytes 786440 | tf_op jit(solution)/shard_map/ppermute | solution.py:53
  170.5 28.7 %copy-start = (f32[2048]{0:T(1024)}, f32[2048]{0:T(1024)S(1)}, u32[]{:S(2)}) copy-start(f32[2048]{0:T(1024)S(1)} %add_multiply_fusion.1) | copy-start | bytes 24580
Sparse Core Ops, SparseCore 0:
  230.8 35.1 all-reduce.1
